TPU v7x, 256 devices: a whole 4x4x8 slice. The times are simulated.
256 devices in a mesh: tm: 128 (over z, y, x), rows: 2 (over core).
Axes of the slice: x: 4, y: 4, z: 8, core: 2. Of those that a mesh axis runs over, the one named last changes fastest.
Arguments:
- band_blocks: float32 [8, 3, 64, 64], replicated, may hold values from 0.1 to 1
- band_offsets: int32 [8, 3], replicated, may hold values from 0 to 7, as said below
- retention: float32 [512], replicated, may hold values from 0.85 to 0.99
- frame_scale: float32 [512, 8], P('tm'), may hold values from 0.95 to 0.999
- sensor_index: int32 [128], replicated, may hold values from 0 to 511, as said below
- sensor_gain: float32 [128], replicated, may hold values from 0.2 to 0.6
- readings: float32 [512, 128], P('tm'), may hold values from -6 to 6
- noise_cov: float32 [512, 512], P(None, 'rows'), may hold values from -0.01 to 0.2
- initial_mean: float32 [512], replicated, may hold values from -6 to 6
- smoother_gain: float32 [512, 512], replicated, may hold values from -0.001 to 1, as said below
Outputs:
- filtered_cov: float32 [128, 512, 512], P('tm', None, 'rows')
- smoothed_means: float32 [512, 512], P('tm', 'rows')
Inputs may be any that keep to these rules, and one draw needn't show every extreme that they name: `band_offsets`: band 0 of block row i names block i; the other bands of a row name distinct other blocks. `sensor_index`: the sensors read distinct nodes. Every eigenvalue of smoother_gain lies inside the unit circle.
All inputs are finite; a program needn't handle non-finite values.
Results may differ from a plain program's by a relative error of at most 0.0003.
Values sent between devices are 32-bit elements; how exact they have to be, the bound alone decides.
No kernel may reach another device: no remote copies, remote signals or barrier semaphores. Data moves between devices by JAX's collectives and lax.ppermute only.
A program may use at most 64 MiB of HBM per device.

v0:
```python
import jax
import jax.numpy as jnp
from jax import lax
from jax.sharding import PartitionSpec as P

HIGHEST_PRECISION = lax.Precision.HIGHEST


def shifted(value, axis, steps):
    count = lax.axis_size(axis)
    leading, last = (max(0, -steps), min(count, count - steps))
    return lax.ppermute(value, axis, [(source, source + steps) for source in range(leading, last)])


def matmul(left, right):
    return jnp.dot(left, right, precision=HIGHEST_PRECISION, preferred_element_type=jnp.float32)


def build_coupling(band_blocks, band_offsets, retention):
    block_count = band_blocks.shape[0]
    block_size = band_blocks.shape[2]
    totals = jnp.sum(band_blocks, axis=(1, 3))
    normed = band_blocks / totals[:, None, :, None]
    placement = (
        band_offsets[:, :, None] == jnp.arange(block_count, dtype=jnp.int32)[None, None, :]
    ).astype(jnp.float32)
    spread_matrix = jnp.einsum("ibj,ibac->iajc", placement, normed, precision=HIGHEST_PRECISION)
    spread_matrix = spread_matrix.reshape(block_count * block_size, block_count * block_size)
    return (1.0 - retention)[:, None] * spread_matrix + jnp.diag(retention)


def matrix_power(square, exponent):
    result = None
    factor = square
    while exponent > 0:
        if exponent % 2 == 1:
            result = factor
        exponent = exponent // 2
        if exponent > 0:
            factor = matmul(factor, factor)
    return result


def local(
    band_blocks,
    band_offsets,
    retention,
    frame_scale,
    sensor_index,
    sensor_gain,
    readings,
    noise_cov,
    initial_mean,
    smoother_gain,
):
    node_count = retention.shape[0]
    block_size = band_blocks.shape[2]
    frames = readings.shape[0]
    panel_width = noise_cov.shape[1]
    tm_devices = lax.axis_size("tm")
    segment = lax.axis_index("tm")
    panel_start = lax.axis_index("rows") * panel_width
    coupling = build_coupling(band_blocks, band_offsets, retention)
    sensor_hit = (sensor_index[:, None] == jnp.arange(node_count, dtype=jnp.int32)[None, :]).astype(
        jnp.float32
    )
    damping = 1.0 - matmul(sensor_gain, sensor_hit)
    inject = matmul(readings * sensor_gain[None, :], sensor_hit)
    anchor = jnp.where(segment == 0, initial_mean, jnp.zeros_like(initial_mean))

    def transition(frame):
        scale_row = lax.dynamic_index_in_dim(frame_scale, frame, 0, keepdims=False)
        return jnp.repeat(scale_row, block_size)[:, None] * coupling

    def injected(frame):
        return lax.dynamic_index_in_dim(inject, frame, 0, keepdims=False)

    first_update = damping[:, None] * transition(0)
    first_offset = matmul(first_update, anchor) + inject[0]
    columns = (
        jnp.arange(node_count, dtype=jnp.int32)[:, None]
        == panel_start + jnp.arange(panel_width, dtype=jnp.int32)[None, :]
    ).astype(jnp.float32)

    def segment_frame(frame, carry):
        chain_cols, offset, cov_cols = carry
        update = damping[:, None] * transition(frame)
        gathered = lax.all_gather(cov_cols, "rows", axis=1, tiled=True)
        update_rows = lax.dynamic_slice_in_dim(update, panel_start, panel_width, 0)
        cov_cols = matmul(update, matmul(gathered, update_rows.T)) + noise_cov
        return (matmul(update, chain_cols), matmul(update, offset) + injected(frame), cov_cols)

    element = lax.fori_loop(
        1, frames, segment_frame, (matmul(first_update, columns), first_offset, noise_cov)
    )

    def combine(succeeding, preceding):
        later_full, earlier_cov = (
            lax.all_gather(succeeding[0], "rows", axis=1, tiled=True),
            lax.all_gather(preceding[2], "rows", axis=1, tiled=True),
        )
        later_rows = lax.dynamic_slice_in_dim(later_full, panel_start, panel_width, 0)
        return (
            matmul(later_full, preceding[0]),
            matmul(later_full, preceding[1]) + succeeding[1],
            matmul(later_full, matmul(earlier_cov, later_rows.T)) + succeeding[2],
        )

    distances = [1] + [
        1 << level for level in range(tm_devices.bit_length()) if 1 << level < tm_devices
    ]
    prefix = element
    for position, stride in enumerate(distances):
        received = shifted((prefix[0], prefix[1], prefix[2]), "tm", stride)
        if position == 0:
            prefix = received
        else:
            merged = combine(prefix, received)
            prefix = tuple(
                (
                    jnp.where(segment >= stride, new_part, old_part)
                    for new_part, old_part in zip(merged, prefix)
                )
            )
    ending = combine(element, prefix)
    cov_out = ending[2][None]
    mean_start = jnp.where(segment == 0, initial_mean, prefix[1])

    def filter_frame(mean_now, frame):
        predicted = matmul(transition(frame), mean_now)
        mean_now = damping * predicted + injected(frame)
        return (mean_now, (mean_now, predicted))

    _, (mean_stack, pred_stack) = lax.scan(
        filter_frame, mean_start, jnp.arange(frames, dtype=jnp.int32)
    )

    def smooth_pass(bracket):

        def frame_back(bracket, inputs):
            mean_now, predicted = inputs
            smooth = mean_now + matmul(smoother_gain, bracket)
            return (smooth - predicted, smooth)

        return lax.scan(frame_back, bracket, (mean_stack, pred_stack), reverse=True)

    own_bracket, _ = smooth_pass(jnp.zeros_like(initial_mean))
    gain_power = matrix_power(smoother_gain, frames)
    suffix = own_bracket
    for position, stride in enumerate(distances):
        received = shifted(suffix, "tm", -stride)
        if position == 0:
            suffix = received
        else:
            suffix = suffix + matmul(gain_power, received)
            gain_power = matmul(gain_power, gain_power)
    _, smoothed = smooth_pass(suffix)
    return (cov_out, lax.dynamic_slice_in_dim(smoothed, panel_start, panel_width, 1))


def solution(mesh):
    return jax.shard_map(
        local,
        mesh=mesh,
        in_specs=(P(), P(), P(), P("tm", None), P(), P(), P("tm", None), P(None, "rows"), P(), P()),
        out_specs=(P("tm", None, "rows"), P("tm", "rows")),
        check_vma=False,
    )
```

profile of v0, /device:TPU:1, one launch (start us, length us, event | category | flops | bytes accessed | tf_op | source)
XLA Modules:
  0.0 583.1 jit_solution(16345871227725126471)
XLA Ops:
  18.0 73.0 %while.66 = (s32[]{:T(128)}, f32[512,256]{1,0:T(8,128)S(1)}, f32[512]{0:T(512)S(1)}, f32[512,256]{1,0:T(8,128)S(1)}, f32[512]{0:T(512)S(1)}, /*index=5*/f32[4,8]...) while((s32[]{:T(128)}, f32[512,256]{1,0:T(8,128)S(1)}, ...), condition=%wide.region_2.3_spmd, body=%wide.region_1.2_spmd.sunk | while | flops 2419720704 | bytes 17850712 | solution.py:93
  21.2 18.8 %all-gather.50.cloned.1.call-done = f32[512,512]{1,0:T(8,128)} async-done(((f32[512,256]{1,0:T(8,128)}), f32[512,512]{1,0:T(8,128)}) %all-gather.50.cloned.1.call-update) | async-done | bytes 1048592 | tf_op jit(solution)/shard_map/while/body/eval_jaxpr/all_gather | solution.py:88
  47.7 15.6 %all-gather.50.cloned.1.call-done = f32[512,512]{1,0:T(8,128)} async-done(((f32[512,256]{1,0:T(8,128)}), f32[512,512]{1,0:T(8,128)}) %all-gather.50.cloned.1.call-update) | async-done | bytes 1048592 | tf_op jit(solution)/shard_map/while/body/eval_jaxpr/all_gather | solution.py:88
  71.0 15.6 %all-gather.50.cloned.1.call-done = f32[512,512]{1,0:T(8,128)} async-done(((f32[512,256]{1,0:T(8,128)}), f32[512,512]{1,0:T(8,128)}) %all-gather.50.cloned.1.call-update) | async-done | bytes 1048592 | tf_op jit(solution)/shard_map/while/body/eval_jaxpr/all_gather | solution.py:88
  97.0 7.9 %collective-permute-done = f32[512,256]{1,0:T(8,128)S(1)} collective-permute-done((f32[512,256]{1,0:T(8,128)S(1)}, f32[512,256]{1,0:T(8,128)S(1)}, u32[]{:S(2)}, u32[]{:S(2)}) %collective-permute-start) | collective-permute-done | bytes 524320 | tf_op jit(solution)/shard_map/ppermute | solution.py:12
  105.8 10.4 %collective-permute-done.7 = f32[512,256]{1,0:T(8,128)S(1)} collective-permute-done((f32[512,256]{1,0:T(8,128)S(1)}, f32[512,256]{1,0:T(8,128)S(1)}, u32[]{:S(2)}, u32[]{:S(2)}) %collective-permute-start.7) | collective-permute-done | bytes 524320 | tf_op jit(solution)/shard_map/ppermute | solution.py:12
  120.3 10.2 %collective-permute-done.8 = f32[512,256]{1,0:T(8,128)S(1)} collective-permute-done((f32[512,256]{1,0:T(8,128)S(1)}, f32[512,256]{1,0:T(8,128)S(1)}, u32[]{:S(2)}, u32[]{:S(2)}) %collective-permute-start.8) | collective-permute-done | bytes 524320 | tf_op jit(solution)/shard_map/ppermute | solution.py:12
  135.5 9.6 %collective-permute-done.1 = f32[512,256]{1,0:T(8,128)S(1)} collective-permute-done((f32[512,256]{1,0:T(8,128)}, f32[512,256]{1,0:T(8,128)S(1)}, u32[]{:S(2)}, u32[]{:S(2)}) %collective-permute-start.1) | collective-permute-done | bytes 524320 | tf_op jit(solution)/shard_map/ppermute | solution.py:12
  149.6 6.3 %all-gather.34.cloned.1.call-done = f32[512,512]{1,0:T(8,128)} async-done(((f32[512,256]{1,0:T(8,128)}), f32[512,512]{1,0:T(8,128)}) %all-gather.34.cloned.1.call-update) | async-done | bytes 1048592 | tf_op jit(solution)/shard_map/all_gather | solution.py:100
  160.0 5.2 collective-permute-start.9
  165.2 10.2 %collective-permute-done.9 = f32[512,256]{1,0:T(8,128)} collective-permute-done((f32[512,256]{1,0:T(8,128)S(1)}, f32[512,256]{1,0:T(8,128)}, u32[]{:S(2)}, u32[]{:S(2)}) %collective-permute-start.9) | collective-permute-done | bytes 524320 | tf_op jit(solution)/shard_map/ppermute | solution.py:12
  175.5 6.5 %collective-permute-start.2 = (f32[512,256]{1,0:T(8,128)S(1)}, f32[512,256]{1,0:T(8,128)}, u32[]{:S(2)}, u32[]{:S(2)}) collective-permute-start(f32[512,256]{1,0:T(8,128)S(1)} %copy-done.14), channel_id=1, source_target_pairs={{0,4},{2,6},{4,8},{6,10},{8,12},{10,14},{12,16},{14,18},{16,20},{1... | collective-permute-start | bytes 1572872 | tf_op jit(solution)/shard_map/ppermute | solution.py:12
  182.1 9.4 %collective-permute-done.2 = f32[512,256]{1,0:T(8,128)} collective-permute-done((f32[512,256]{1,0:T(8,128)S(1)}, f32[512,256]{1,0:T(8,128)}, u32[]{:S(2)}, u32[]{:S(2)}) %collective-permute-start.2) | collective-permute-done | bytes 524320 | tf_op jit(solution)/shard_map/ppermute | solution.py:12
  194.7 9.0 %all-gather.36.cloned.1.call-done = f32[512,512]{1,0:T(8,128)} async-done(((f32[512,256]{1,0:T(8,128)}), f32[512,512]{1,0:T(8,128)}) %all-gather.36.cloned.1.call-update) | async-done | bytes 1048592 | tf_op jit(solution)/shard_map/all_gather | solution.py:100
  211.7 10.3 %collective-permute-done.10 = f32[512,256]{1,0:T(8,128)} collective-permute-done((f32[512,256]{1,0:T(8,128)S(1)}, f32[512,256]{1,0:T(8,128)}, u32[]{:S(2)}, u32[]{:S(2)}) %collective-permute-start.10) | collective-permute-done | bytes 524320 | tf_op jit(solution)/shard_map/ppermute | solution.py:12
  227.1 9.4 %collective-permute-done.3 = f32[512,256]{1,0:T(8,128)} collective-permute-done((f32[512,256]{1,0:T(8,128)S(1)}, f32[512,256]{1,0:T(8,128)}, u32[]{:S(2)}, u32[]{:S(2)}) %collective-permute-start.3) | collective-permute-done | bytes 524320 | tf_op jit(solution)/shard_map/ppermute | solution.py:12
  239.7 5.3 all-gather.38.cloned.1.call-done
  249.3 5.2 collective-permute-start.11
  254.6 10.2 %collective-permute-done.11 = f32[512,256]{1,0:T(8,128)} collective-permute-done((f32[512,256]{1,0:T(8,128)S(1)}, f32[512,256]{1,0:T(8,128)}, u32[]{:S(2)}, u32[]{:S(2)}) %collective-permute-start.11) | collective-permute-done | bytes 524320 | tf_op jit(solution)/shard_map/ppermute | solution.py:12
  264.9 6.5 %collective-permute-start.4 = (f32[512,256]{1,0:T(8,128)S(1)}, f32[512,256]{1,0:T(8,128)}, u32[]{:S(2)}, u32[]{:S(2)}) collective-permute-start(f32[512,256]{1,0:T(8,128)S(1)} %copy-done.15), channel_id=1, source_target_pairs={{0,16},{2,18},{4,20},{6,22},{8,24},{10,26},{12,28},{14,30},{16,32}... | collective-permute-start | bytes 1572872 | tf_op jit(solution)/shard_map/ppermute | solution.py:12
  271.4 9.4 %collective-permute-done.4 = f32[512,256]{1,0:T(8,128)} collective-permute-done((f32[512,256]{1,0:T(8,128)S(1)}, f32[512,256]{1,0:T(8,128)}, u32[]{:S(2)}, u32[]{:S(2)}) %collective-permute-start.4) | collective-permute-done | bytes 524320 | tf_op jit(solution)/shard_map/ppermute | solution.py:12
  289.1 6.6 %collective-permute-start.12 = (f32[512,256]{1,0:T(8,128)S(1)}, f32[512,256]{1,0:T(8,128)}, u32[]{:S(2)}, u32[]{:S(2)}) collective-permute-start(f32[512,256]{1,0:T(8,128)S(1)} %fusion.11), channel_id=1, source_target_pairs={{0,32},{2,34},{4,36},{6,38},{8,40},{10,42},{12,44},{14,46},{16,48}... | collective-permute-start | bytes 1572872 | tf_op jit(solution)/shard_map/ppermute | solution.py:12
  295.6 8.5 %collective-permute-done.12 = f32[512,256]{1,0:T(8,128)} collective-permute-done((f32[512,256]{1,0:T(8,128)S(1)}, f32[512,256]{1,0:T(8,128)}, u32[]{:S(2)}, u32[]{:S(2)}) %collective-permute-start.12) | collective-permute-done | bytes 524320 | tf_op jit(solution)/shard_map/ppermute | solution.py:12
  309.3 7.7 %collective-permute-done.5 = f32[512,256]{1,0:T(8,128)} collective-permute-done((f32[512,256]{1,0:T(8,128)S(1)}, f32[512,256]{1,0:T(8,128)}, u32[]{:S(2)}, u32[]{:S(2)}) %collective-permute-start.5) | collective-permute-done | bytes 524320 | tf_op jit(solution)/shard_map/ppermute | solution.py:12
  320.2 5.6 all-gather.42.cloned.1.call-done
  346.3 29.4 %collective-permute-start.6 = (f32[512,256]{1,0:T(8,128)S(1)}, f32[512,256]{1,0:T(8,128)S(1)}, u32[]{:S(2)}, u32[]{:S(2)}) collective-permute-start(f32[512,256]{1,0:T(8,128)S(1)} %copy-done.13), channel_id=1, source_target_pairs={{0,64},{2,66},{4,68},{6,70},{8,72},{10,74},{12,76},{14,78},{16,80}... | collective-permute-start | bytes 1572872 | tf_op jit(solution)/shard_map/ppermute | solution.py:12
  392.9 15.9 %collective-permute-start.14 = (f32[512,256]{1,0:T(8,128)S(1)}, f32[512,256]{1,0:T(8,128)}, u32[]{:S(2)}, u32[]{:S(2)}) collective-permute-start(f32[512,256]{1,0:T(8,128)S(1)} %fusion.9), channel_id=1, source_target_pairs={{0,128},{2,130},{4,132},{6,134},{8,136},{10,138},{12,140},{14,142}... | collective-permute-start | bytes 1572872 | tf_op jit(solution)/shard_map/ppermute | solution.py:12
  421.1 16.1 %collective-permute-start.21 = (f32[512]{0:T(512)S(1)}, f32[512]{0:T(512)S(1)}, u32[]{:S(2)}, u32[]{:S(2)}) collective-permute-start(f32[512]{0:T(512)S(1)} %add_select_fusion.2), channel_id=1, source_target_pairs={{0,64},{2,66},{4,68},{6,70},{8,72},{10,74},{12,76},{14,78},{16,80}... | collective-permute-start | bytes 6152 | tf_op jit(solution)/shard_map/ppermute | solution.py:12
  440.2 8.2 %collective-permute-start.22 = (f32[512]{0:T(512)S(1)}, f32[512]{0:T(512)S(1)}, u32[]{:S(2)}, u32[]{:S(2)}) collective-permute-start(f32[512]{0:T(512)S(1)} %add_select_fusion.1), channel_id=1, source_target_pairs={{0,128},{2,130},{4,132},{6,134},{8,136},{10,138},{12,140},{14,142}... | collective-permute-start | bytes 6152 | tf_op jit(solution)/shard_map/ppermute | solution.py:12
  451.4 15.8 %while.67 = (s32[]{:T(128)}, f32[512]{0:T(512)S(1)}, f32[4,512]{1,0:T(4,128)S(1)}, f32[4,512]{1,0:T(4,128)S(1)}, s32[4]{0:T(128)S(1)}, /*index=5*/f32[4,8]{1,0:T...) while((s32[]{:T(128)}, f32[512]{0:T(512)S(1)}, ...), condition=%wide.region_4.5_spmd, body=%wide.region_3.4_spmd.sunk | while | flops 3408901 | bytes 1081619 | solution.py:134
  496.3 5.9 %collective-permute-done.27 = f32[512]{0:T(512)S(1)} collective-permute-done((f32[512]{0:T(512)S(1)}, f32[512]{0:T(512)S(1)}, u32[]{:S(2)}, u32[]{:S(2)}) %collective-permute-start.27) | collective-permute-done | bytes 2080 | tf_op jit(solution)/shard_map/ppermute | solution.py:12
  537.5 33.6 %all-gather.48.cloned.1.call-done = f32[512,512]{1,0:T(8,128)} async-done(((f32[512,256]{1,0:T(8,128)}), f32[512,512]{1,0:T(8,128)}) %all-gather.48.cloned.1.call-update) | async-done | bytes 1048592 | tf_op jit(solution)/shard_map/all_gather | solution.py:100
  (360 shorter events, 237.5 us)
Async XLA Ops:
  18.0 22.1 %all-gather.50.cloned.1.call-start = ((), (), s32[]{:S(2)}) async-start(), calls=%async_computation.16 | async-start | bytes 1572864 | tf_op jit(solution)/shard_map/while/body/eval_jaxpr/all_gather | solution.py:88
  44.5 18.9 %all-gather.50.cloned.1.call-start = ((), (), s32[]{:S(2)}) async-start(), calls=%async_computation.16 | async-start | bytes 1572864 | tf_op jit(solution)/shard_map/while/body/eval_jaxpr/all_gather | solution.py:88
  67.7 18.9 %all-gather.50.cloned.1.call-start = ((), (), s32[]{:S(2)}) async-start(), calls=%async_computation.16 | async-start | bytes 1572864 | tf_op jit(solution)/shard_map/while/body/eval_jaxpr/all_gather | solution.py:88
  91.0 54.9 %all-gather.20.cloned.1.call-start = ((), (), s32[]{:S(2)}) async-start(), calls=%async_computation.1 | async-start | bytes 1572864 | tf_op jit(solution)/shard_map/all_gather | solution.py:99
  93.9 22.2 %collective-permute-start.7 = (f32[512,256]{1,0:T(8,128)S(1)}, f32[512,256]{1,0:T(8,128)S(1)}, u32[]{:S(2)}, u32[]{:S(2)}) collective-permute-start(f32[512,256]{1,0:T(8,128)S(1)} %get-tuple-element.586), channel_id=1, source_target_pairs={{0,2},{2,4},{4,6},{6,8},{8,10},{10,12},{12,14},{14,16},{16,18},{18... | collective-permute-start | bytes 1572872 | tf_op jit(solution)/shard_map/ppermute | solution.py:12
  105.8 50.2 %all-gather.34.cloned.1.call-start = ((), (), s32[]{:S(2)}) async-start(), calls=%async_computation.8 | async-start | bytes 1572864 | tf_op jit(solution)/shard_map/all_gather | solution.py:100
  116.2 14.3 %collective-permute-start.8 = (f32[512,256]{1,0:T(8,128)S(1)}, f32[512,256]{1,0:T(8,128)S(1)}, u32[]{:S(2)}, u32[]{:S(2)}) collective-permute-start(f32[512,256]{1,0:T(8,128)S(1)} %collective-permute-done.7), channel_id=1, source_target_pairs={{0,2},{2,4},{4,6},{6,8},{8,10},{10,12},{12,14},{14,16},{16,18},{18... | collective-permute-start | bytes 1572872 | tf_op jit(solution)/shard_map/ppermute | solution.py:12
  131.3 60.2 %all-gather.22.cloned.1.call-start = ((), (), s32[]{:S(2)}) async-start(), calls=%async_computation.2 | async-start | bytes 1572864 | tf_op jit(solution)/shard_map/all_gather | solution.py:99
  149.3 54.4 %all-gather.36.cloned.1.call-start = ((), (), s32[]{:S(2)}) async-start(), calls=%async_computation.9 | async-start | bytes 1572864 | tf_op jit(solution)/shard_map/all_gather | solution.py:100
  160.0 15.4 %collective-permute-start.9 = (f32[512,256]{1,0:T(8,128)S(1)}, f32[512,256]{1,0:T(8,128)}, u32[]{:S(2)}, u32[]{:S(2)}) collective-permute-start(f32[512,256]{1,0:T(8,128)S(1)} %fusion.14), channel_id=1, source_target_pairs={{0,4},{2,6},{4,8},{6,10},{8,12},{10,14},{12,16},{14,18},{16,20},{1... | collective-permute-start | bytes 1572872 | tf_op jit(solution)/shard_map/ppermute | solution.py:12
  175.5 61.0 %all-gather.24.cloned.1.call-start = ((), (), s32[]{:S(2)}) async-start(), calls=%async_computation.3 | async-start | bytes 1572864 | tf_op jit(solution)/shard_map/all_gather | solution.py:99
  175.5 15.9 %collective-permute-start.2 = (f32[512,256]{1,0:T(8,128)S(1)}, f32[512,256]{1,0:T(8,128)}, u32[]{:S(2)}, u32[]{:S(2)}) collective-permute-start(f32[512,256]{1,0:T(8,128)S(1)} %copy-done.14), channel_id=1, source_target_pairs={{0,4},{2,6},{4,8},{6,10},{8,12},{10,14},{12,16},{14,18},{16,20},{1... | collective-permute-start | bytes 1572872 | tf_op jit(solution)/shard_map/ppermute | solution.py:12
  194.6 50.3 %all-gather.38.cloned.1.call-start = ((), (), s32[]{:S(2)}) async-start(), calls=%async_computation.10 | async-start | bytes 1572864 | tf_op jit(solution)/shard_map/all_gather | solution.py:100
  222.0 58.8 %all-gather.26.cloned.1.call-start = ((), (), s32[]{:S(2)}) async-start(), calls=%async_computation.4 | async-start | bytes 1572864 | tf_op jit(solution)/shard_map/all_gather | solution.py:99
  222.1 14.4 %collective-permute-start.3 = (f32[512,256]{1,0:T(8,128)S(1)}, f32[512,256]{1,0:T(8,128)}, u32[]{:S(2)}, u32[]{:S(2)}) collective-permute-start(f32[512,256]{1,0:T(8,128)S(1)} %copy-done.17), channel_id=1, source_target_pairs={{0,8},{2,10},{4,12},{6,14},{8,16},{10,18},{12,20},{14,22},{16,24},... | collective-permute-start | bytes 1572872 | tf_op jit(solution)/shard_map/ppermute | solution.py:12
  239.7 45.1 %all-gather.40.cloned.1.call-start = ((), (), s32[]{:S(2)}) async-start(), calls=%async_computation.11 | async-start | bytes 1572864 | tf_op jit(solution)/shard_map/all_gather | solution.py:100
  249.3 15.4 %collective-permute-start.11 = (f32[512,256]{1,0:T(8,128)S(1)}, f32[512,256]{1,0:T(8,128)}, u32[]{:S(2)}, u32[]{:S(2)}) collective-permute-start(f32[512,256]{1,0:T(8,128)S(1)} %fusion.12), channel_id=1, source_target_pairs={{0,16},{2,18},{4,20},{6,22},{8,24},{10,26},{12,28},{14,30},{16,32}... | collective-permute-start | bytes 1572872 | tf_op jit(solution)/shard_map/ppermute | solution.py:12
  264.8 52.2 %all-gather.28.cloned.1.call-start = ((), (), s32[]{:S(2)}) async-start(), calls=%async_computation.5 | async-start | bytes 1572864 | tf_op jit(solution)/shard_map/all_gather | solution.py:99
  264.9 15.9 %collective-permute-start.4 = (f32[512,256]{1,0:T(8,128)S(1)}, f32[512,256]{1,0:T(8,128)}, u32[]{:S(2)}, u32[]{:S(2)}) collective-permute-start(f32[512,256]{1,0:T(8,128)S(1)} %copy-done.15), channel_id=1, source_target_pairs={{0,16},{2,18},{4,20},{6,22},{8,24},{10,26},{12,28},{14,30},{16,32}... | collective-permute-start | bytes 1572872 | tf_op jit(solution)/shard_map/ppermute | solution.py:12
  284.1 41.8 %all-gather.42.cloned.1.call-start = ((), (), s32[]{:S(2)}) async-start(), calls=%async_computation.12 | async-start | bytes 1572864 | tf_op jit(solution)/shard_map/all_gather | solution.py:100
  289.1 15.1 %collective-permute-start.12 = (f32[512,256]{1,0:T(8,128)S(1)}, f32[512,256]{1,0:T(8,128)}, u32[]{:S(2)}, u32[]{:S(2)}) collective-permute-start(f32[512,256]{1,0:T(8,128)S(1)} %fusion.11), channel_id=1, source_target_pairs={{0,32},{2,34},{4,36},{6,38},{8,40},{10,42},{12,44},{14,46},{16,48}... | collective-permute-start | bytes 1572872 | tf_op jit(solution)/shard_map/ppermute | solution.py:12
  304.2 80.8 %all-gather.30.cloned.1.call-start = ((), (), s32[]{:S(2)}) async-start(), calls=%async_computation.6 | async-start | bytes 1572864 | tf_op jit(solution)/shard_map/all_gather | solution.py:99
  320.1 68.0 %all-gather.44.cloned.1.call-start = ((), (), s32[]{:S(2)}) async-start(), calls=%async_computation.13 | async-start | bytes 1572864 | tf_op jit(solution)/shard_map/all_gather | solution.py:100
  330.2 15.0 %collective-permute-start.13 = (f32[512,256]{1,0:T(8,128)S(1)}, f32[512,256]{1,0:T(8,128)}, u32[]{:S(2)}, u32[]{:S(2)}) collective-permute-start(f32[512,256]{1,0:T(8,128)S(1)} %fusion.10), channel_id=1, source_target_pairs={{0,64},{2,66},{4,68},{6,70},{8,72},{10,74},{12,76},{14,78},{16,80}... | collective-permute-start | bytes 1572872 | tf_op jit(solution)/shard_map/ppermute | solution.py:12
  345.2 103.9 %all-gather.32.cloned.1.call-start = ((), (), s32[]{:S(2)}) async-start(), calls=%async_computation.7 | async-start | bytes 1572864 | tf_op jit(solution)/shard_map/all_gather | solution.py:99
  346.3 38.8 %collective-permute-start.6 = (f32[512,256]{1,0:T(8,128)S(1)}, f32[512,256]{1,0:T(8,128)S(1)}, u32[]{:S(2)}, u32[]{:S(2)}) collective-permute-start(f32[512,256]{1,0:T(8,128)S(1)} %copy-done.13), channel_id=1, source_target_pairs={{0,64},{2,66},{4,68},{6,70},{8,72},{10,74},{12,76},{14,78},{16,80}... | collective-permute-start | bytes 1572872 | tf_op jit(solution)/shard_map/ppermute | solution.py:12
  380.0 28.8 %collective-permute-start.18 = (f32[512]{0:T(512)S(1)}, f32[512]{0:T(512)S(1)}, u32[]{:S(2)}, u32[]{:S(2)}) collective-permute-start(f32[512]{0:T(512)S(1)} %add_select_fusion.5), channel_id=1, source_target_pairs={{0,8},{2,10},{4,12},{6,14},{8,16},{10,18},{12,20},{14,22},{16,24},... | collective-permute-start | bytes 6152 | tf_op jit(solution)/shard_map/ppermute | solution.py:12
  388.1 140.4 %all-gather.46.cloned.1.call-start = ((), (), s32[]{:S(2)}) async-start(), calls=%async_computation.14 | async-start | bytes 1572864 | tf_op jit(solution)/shard_map/all_gather | solution.py:100
  392.9 23.9 %collective-permute-start.14 = (f32[512,256]{1,0:T(8,128)S(1)}, f32[512,256]{1,0:T(8,128)}, u32[]{:S(2)}, u32[]{:S(2)}) collective-permute-start(f32[512,256]{1,0:T(8,128)S(1)} %fusion.9), channel_id=1, source_target_pairs={{0,128},{2,130},{4,132},{6,134},{8,136},{10,138},{12,140},{14,142}... | collective-permute-start | bytes 1572872 | tf_op jit(solution)/shard_map/ppermute | solution.py:12
  416.8 120.7 %all-gather.18.cloned.1.call-start = ((), (), s32[]{:S(2)}) async-start(), calls=%async_computation | async-start | bytes 1572864 | tf_op jit(solution)/shard_map/all_gather | solution.py:99
  421.1 16.9 %collective-permute-start.21 = (f32[512]{0:T(512)S(1)}, f32[512]{0:T(512)S(1)}, u32[]{:S(2)}, u32[]{:S(2)}) collective-permute-start(f32[512]{0:T(512)S(1)} %add_select_fusion.2), channel_id=1, source_target_pairs={{0,64},{2,66},{4,68},{6,70},{8,72},{10,74},{12,76},{14,78},{16,80}... | collective-permute-start | bytes 6152 | tf_op jit(solution)/shard_map/ppermute | solution.py:12
  448.4 122.8 %all-gather.48.cloned.1.call-start = ((), (), s32[]{:S(2)}) async-start(), calls=%async_computation.15 | async-start | bytes 1572864 | tf_op jit(solution)/shard_map/all_gather | solution.py:100
  (60 other events, 465.8 us)
Sparse Core Ops, SparseCore 0:
  21.2 18.8 all-gather.49
  47.7 15.6 all-gather.49
  70.9 15.6 all-gather.49
Sparse Core Ops, SparseCore 1:
  105.8 18.9 all-gather.19
  131.4 24.5 all-gather.33
  157.6 22.3 all-gather.21
  181.8 21.9 all-gather.35
  205.5 19.8 all-gather.23
  227.2 17.7 all-gather.37
  246.7 16.0 all-gather.25
  264.9 19.8 all-gather.39
  286.4 18.9 all-gather.27
  307.2 18.6 all-gather.41
  327.5 16.3 all-gather.29
  345.6 36.4 all-gather.43
  388.2 24.7 all-gather.31
  416.9 26.1 all-gather.45
  448.5 15.5 all-gather.17
  532.7 38.4 all-gather.47
where the time goes:
time: 593 us; the launch traced here: 583 us
  waiting for transfers between devices  261 us (44%)
  starting transfers between devices  157 us (26%)
  matrix products  120 us (20%)
  between operations  17 us (3%)
  local copies, waits for them, and re-layouts  15.7 us (3%)
  loops' own time  8.32 us (1%)
    ppermute x31, starting transfers between devices, shifted(): lax.ppermute(value, axis, [(source, source + steps) for source in range(l...  155 us
    ppermute x31, waiting for transfers between devices, shifted(): lax.ppermute(value, axis, [(source, source + steps) for source in range(l...  150 us
    dot_general x72, matrix products, matmul(): jnp.dot(left, right, precision=HIGHEST_PRECISION, preferred_element_type=...  118 us
    all_gather x8, waiting for transfers between devices, combine(): lax.all_gather(preceding[2], 'rows', axis=1, tiled=True)  60.2 us
    all_gather x3, waiting for transfers between devices, segment_frame(): gathered = lax.all_gather(cov_cols, 'rows', axis=1, tiled=True)  50.1 us
  transfers between devices with their start and end apart: 50, of which 38 were waited for; matrix products, arithmetic and copies ran while one was open for 18% of the time, Pallas kernels for 0%

commit v1 on v0

--- a/solution.py
+++ b/solution.py
@@ -4,6 +4,15 @@
 from jax.sharding import PartitionSpec as P
 
 HIGHEST_PRECISION = lax.Precision.HIGHEST
+quotas_move = lambda arr: jnp.concatenate(
+    jax.lax.all_to_all(
+        jnp.stack([arr] * jax.lax.axis_size("rows"), axis=0),
+        axis_name="rows",
+        split_axis=0,
+        concat_axis=0,
+    ),
+    1,
+)
 
 
 def shifted(value, axis, steps):
@@ -85,7 +94,7 @@
     def segment_frame(frame, carry):
         chain_cols, offset, cov_cols = carry
         update = damping[:, None] * transition(frame)
-        gathered = lax.all_gather(cov_cols, "rows", axis=1, tiled=True)
+        gathered = quotas_move(cov_cols)
         update_rows = lax.dynamic_slice_in_dim(update, panel_start, panel_width, 0)
         cov_cols = matmul(update, matmul(gathered, update_rows.T)) + noise_cov
         return (matmul(update, chain_cols), matmul(update, offset) + injected(frame), cov_cols)

time: 593 us -> 563 us (0.949)
  waiting for transfers between devices: 261 us -> 216 us
  starting transfers between devices: 157 us -> 167 us
    all_gather x3 -> x0, waiting for transfers between devices: 50.1 us -> none  [segment_frame(): gathered = lax.all_gather(cov_cols, 'rows', axis=1, tiled=True)]
    all_to_all x0 -> x3, starting transfers between devices: none -> 14 us  [jax.lax.all_to_all(jnp.stack([arr] * jax.lax.axis_size('rows'), axis=0),...]
  transfers between devices with their start and end apart: 50 -> 50, of which waited for: 38 -> 34; matrix products, arithmetic and copies ran while one was open for 18% -> 19% of each run, Pallas kernels for 0% -> 0%
where the time goes in v1:
time: 563 us; the launch traced here: 553 us
  waiting for transfers between devices  216 us (38%)
  starting transfers between devices  167 us (30%)
  matrix products  118 us (21%)
  local copies, waits for them, and re-layouts  21.5 us (4%)
  between operations  15.3 us (3%)
  other arithmetic  8.25 us (1%)
  loops' own time  7.39 us (1%)
    ppermute x31, waiting for transfers between devices, shifted(): lax.ppermute(value, axis, [(source, source + steps) for source in range(l...  155 us
    ppermute x31, starting transfers between devices, shifted(): lax.ppermute(value, axis, [(source, source + steps) for source in range(l...  151 us
    dot_general x72, matrix products, matmul(): jnp.dot(left, right, precision=HIGHEST_PRECISION, preferred_element_type=...  116 us
    all_gather x8, waiting for transfers between devices, combine(): lax.all_gather(preceding[2], 'rows', axis=1, tiled=True)  60.9 us
    all_to_all x3, starting transfers between devices, jax.lax.all_to_all(jnp.stack([arr] * jax.lax.axis_size('rows'), axis=0),...  14 us
  transfers between devices with their start and end apart: 50, of which 34 were waited for; matrix products, arithmetic and copies ran while one was open for 19% of the time, Pallas kernels for 0%

profile of v1, /device:TPU:1, one launch (start us, length us, event | category | flops | bytes accessed | tf_op | source)
XLA Modules:
  0.0 553.2 jit_solution(16045541849283404261)
XLA Ops:
  18.7 44.5 %while.66 = (s32[]{:T(128)}, f32[512,256]{1,0:T(8,128)}, f32[512]{0:T(512)S(1)}, f32[512,256]{1,0:T(8,128)}, f32[512]{0:T(512)S(1)}, /*index=5*/f32[4,8]{1,0:T(4...) while((s32[]{:T(128)}, f32[512,256]{1,0:T(8,128)}, ...), condition=%wide.region_2.3_spmd, body=%wide.region_1.2_spmd.sunk | while | flops 2419982848 | bytes 18899280 | solution.py:102
  21.1 6.8 %all-to-all-start = ((f32[2,512,256]{1,2,0:T(8,128)}), f32[2,512,256]{1,2,0:T(8,128)S(1)}, u32[]{:S(2)}, u32[]{:S(2)}) async-start(f32[2,512,256]{1,2,0:T(8,128)} %pad_maximum_fusion.2), calls=%async_computation | async-start | bytes 2097152 | tf_op jit(solution)/shard_map/while/body/eval_jaxpr/all_to_all | solution.py:8
  67.8 8.4 %collective-permute-done = f32[512,256]{1,0:T(8,128)S(1)} collective-permute-done((f32[512,256]{1,0:T(8,128)}, f32[512,256]{1,0:T(8,128)S(1)}, u32[]{:S(2)}, u32[]{:S(2)}) %collective-permute-start) | collective-permute-done | bytes 524320 | tf_op jit(solution)/shard_map/ppermute | solution.py:21
  77.0 10.4 %collective-permute-done.7 = f32[512,256]{1,0:T(8,128)S(1)} collective-permute-done((f32[512,256]{1,0:T(8,128)}, f32[512,256]{1,0:T(8,128)S(1)}, u32[]{:S(2)}, u32[]{:S(2)}) %collective-permute-start.7) | collective-permute-done | bytes 524320 | tf_op jit(solution)/shard_map/ppermute | solution.py:21
  91.4 10.3 %collective-permute-done.8 = f32[512,256]{1,0:T(8,128)S(1)} collective-permute-done((f32[512,256]{1,0:T(8,128)S(1)}, f32[512,256]{1,0:T(8,128)S(1)}, u32[]{:S(2)}, u32[]{:S(2)}) %collective-permute-start.8) | collective-permute-done | bytes 524320 | tf_op jit(solution)/shard_map/ppermute | solution.py:21
  106.8 9.8 %collective-permute-done.1 = f32[512,256]{1,0:T(8,128)S(1)} collective-permute-done((f32[512,256]{1,0:T(8,128)}, f32[512,256]{1,0:T(8,128)S(1)}, u32[]{:S(2)}, u32[]{:S(2)}) %collective-permute-start.1) | collective-permute-done | bytes 524320 | tf_op jit(solution)/shard_map/ppermute | solution.py:21
  120.1 8.5 %all-gather.33.cloned.1.call-done = f32[512,512]{1,0:T(8,128)} async-done(((f32[512,256]{1,0:T(8,128)}), f32[512,512]{1,0:T(8,128)}) %all-gather.33.cloned.1.call-update) | async-done | bytes 1048592 | tf_op jit(solution)/shard_map/all_gather | solution.py:109
  137.0 11.0 %collective-permute-done.9 = f32[512,256]{1,0:T(8,128)S(1)} collective-permute-done((f32[512,256]{1,0:T(8,128)S(1)}, f32[512,256]{1,0:T(8,128)S(1)}, u32[]{:S(2)}, u32[]{:S(2)}) %collective-permute-start.9) | collective-permute-done | bytes 524320 | tf_op jit(solution)/shard_map/ppermute | solution.py:21
  148.9 5.6 %collective-permute-start.2 = (f32[512,256]{1,0:T(8,128)S(1)}, f32[512,256]{1,0:T(8,128)S(1)}, u32[]{:S(2)}, u32[]{:S(2)}) collective-permute-start(f32[512,256]{1,0:T(8,128)S(1)} %copy-done.14), channel_id=1, source_target_pairs={{0,4},{2,6},{4,8},{6,10},{8,12},{10,14},{12,16},{14,18},{16,20},{1... | collective-permute-start | bytes 1572872 | tf_op jit(solution)/shard_map/ppermute | solution.py:21
  154.6 10.2 %collective-permute-done.2 = f32[512,256]{1,0:T(8,128)S(1)} collective-permute-done((f32[512,256]{1,0:T(8,128)S(1)}, f32[512,256]{1,0:T(8,128)S(1)}, u32[]{:S(2)}, u32[]{:S(2)}) %collective-permute-start.2) | collective-permute-done | bytes 524320 | tf_op jit(solution)/shard_map/ppermute | solution.py:21
  169.1 7.4 %all-gather.35.cloned.1.call-done = f32[512,512]{1,0:T(8,128)} async-done(((f32[512,256]{1,0:T(8,128)}), f32[512,512]{1,0:T(8,128)}) %all-gather.35.cloned.1.call-update) | async-done | bytes 1048592 | tf_op jit(solution)/shard_map/all_gather | solution.py:109
  184.3 10.2 %collective-permute-done.10 = f32[512,256]{1,0:T(8,128)} collective-permute-done((f32[512,256]{1,0:T(8,128)S(1)}, f32[512,256]{1,0:T(8,128)}, u32[]{:S(2)}, u32[]{:S(2)}) %collective-permute-start.10) | collective-permute-done | bytes 524320 | tf_op jit(solution)/shard_map/ppermute | solution.py:21
  194.6 5.0 collective-permute-start.3
  199.6 9.7 %collective-permute-done.3 = f32[512,256]{1,0:T(8,128)} collective-permute-done((f32[512,256]{1,0:T(8,128)}, f32[512,256]{1,0:T(8,128)}, u32[]{:S(2)}, u32[]{:S(2)}) %collective-permute-start.3) | collective-permute-done | bytes 524320 | tf_op jit(solution)/shard_map/ppermute | solution.py:21
  212.7 6.0 %all-gather.37.cloned.1.call-done = f32[512,512]{1,0:T(8,128)} async-done(((f32[512,256]{1,0:T(8,128)}), f32[512,512]{1,0:T(8,128)}) %all-gather.37.cloned.1.call-update) | async-done | bytes 1048592 | tf_op jit(solution)/shard_map/all_gather | solution.py:109
  223.0 5.2 collective-permute-start.11
  228.2 10.2 %collective-permute-done.11 = f32[512,256]{1,0:T(8,128)} collective-permute-done((f32[512,256]{1,0:T(8,128)S(1)}, f32[512,256]{1,0:T(8,128)}, u32[]{:S(2)}, u32[]{:S(2)}) %collective-permute-start.11) | collective-permute-done | bytes 524320 | tf_op jit(solution)/shard_map/ppermute | solution.py:21
  238.5 6.5 %collective-permute-start.4 = (f32[512,256]{1,0:T(8,128)}, f32[512,256]{1,0:T(8,128)}, u32[]{:S(2)}, u32[]{:S(2)}) collective-permute-start(f32[512,256]{1,0:T(8,128)} %convolution_select_fusion.3), channel_id=1, source_target_pairs={{0,16},{2,18},{4,20},{6,22},{8,24},{10,26},{12,28},{14,30},{16,32}... | collective-permute-start | bytes 1572872 | tf_op jit(solution)/shard_map/ppermute | solution.py:21
  245.0 9.7 %collective-permute-done.4 = f32[512,256]{1,0:T(8,128)} collective-permute-done((f32[512,256]{1,0:T(8,128)}, f32[512,256]{1,0:T(8,128)}, u32[]{:S(2)}, u32[]{:S(2)}) %collective-permute-start.4) | collective-permute-done | bytes 524320 | tf_op jit(solution)/shard_map/ppermute | solution.py:21
  263.0 6.5 %collective-permute-start.12 = (f32[512,256]{1,0:T(8,128)S(1)}, f32[512,256]{1,0:T(8,128)}, u32[]{:S(2)}, u32[]{:S(2)}) collective-permute-start(f32[512,256]{1,0:T(8,128)S(1)} %fusion.11), channel_id=1, source_target_pairs={{0,32},{2,34},{4,36},{6,38},{8,40},{10,42},{12,44},{14,46},{16,48}... | collective-permute-start | bytes 1572872 | tf_op jit(solution)/shard_map/ppermute | solution.py:21
  269.5 8.5 %collective-permute-done.12 = f32[512,256]{1,0:T(8,128)} collective-permute-done((f32[512,256]{1,0:T(8,128)S(1)}, f32[512,256]{1,0:T(8,128)}, u32[]{:S(2)}, u32[]{:S(2)}) %collective-permute-start.12) | collective-permute-done | bytes 524320 | tf_op jit(solution)/shard_map/ppermute | solution.py:21
  278.1 5.0 collective-permute-start.5
  283.1 8.0 %collective-permute-done.5 = f32[512,256]{1,0:T(8,128)} collective-permute-done((f32[512,256]{1,0:T(8,128)}, f32[512,256]{1,0:T(8,128)}, u32[]{:S(2)}, u32[]{:S(2)}) %collective-permute-start.5) | collective-permute-done | bytes 524320 | tf_op jit(solution)/shard_map/ppermute | solution.py:21
  294.5 5.3 all-gather.41.cloned.1.call-done
  320.3 29.6 %collective-permute-start.6 = (f32[512,256]{1,0:T(8,128)}, f32[512,256]{1,0:T(8,128)S(1)}, u32[]{:S(2)}, u32[]{:S(2)}) collective-permute-start(f32[512,256]{1,0:T(8,128)} %convolution_select_fusion.1), channel_id=1, source_target_pairs={{0,64},{2,66},{4,68},{6,70},{8,72},{10,74},{12,76},{14,78},{16,80}... | collective-permute-start | bytes 1572872 | tf_op jit(solution)/shard_map/ppermute | solution.py:21
  354.2 5.6 %collective-permute-done.6 = f32[512,256]{1,0:T(8,128)S(1)} collective-permute-done((f32[512,256]{1,0:T(8,128)}, f32[512,256]{1,0:T(8,128)S(1)}, u32[]{:S(2)}, u32[]{:S(2)}) %collective-permute-start.6) | collective-permute-done | bytes 524320 | tf_op jit(solution)/shard_map/ppermute | solution.py:21
  367.8 14.1 %collective-permute-start.14 = (f32[512,256]{1,0:T(8,128)S(1)}, f32[512,256]{1,0:T(8,128)}, u32[]{:S(2)}, u32[]{:S(2)}) collective-permute-start(f32[512,256]{1,0:T(8,128)S(1)} %fusion.9), channel_id=1, source_target_pairs={{0,128},{2,130},{4,132},{6,134},{8,136},{10,138},{12,140},{14,142}... | collective-permute-start | bytes 1572872 | tf_op jit(solution)/shard_map/ppermute | solution.py:21
  395.2 13.9 %collective-permute-start.21 = (f32[512]{0:T(512)S(1)}, f32[512]{0:T(512)S(1)}, u32[]{:S(2)}, u32[]{:S(2)}) collective-permute-start(f32[512]{0:T(512)S(1)} %add_select_fusion.2), channel_id=1, source_target_pairs={{0,64},{2,66},{4,68},{6,70},{8,72},{10,74},{12,76},{14,78},{16,80}... | collective-permute-start | bytes 6152 | tf_op jit(solution)/shard_map/ppermute | solution.py:21
  412.0 8.1 %collective-permute-start.22 = (f32[512]{0:T(512)S(1)}, f32[512]{0:T(512)S(1)}, u32[]{:S(2)}, u32[]{:S(2)}) collective-permute-start(f32[512]{0:T(512)S(1)} %add_select_fusion.1), channel_id=1, source_target_pairs={{0,128},{2,130},{4,132},{6,134},{8,136},{10,138},{12,140},{14,142}... | collective-permute-start | bytes 6152 | tf_op jit(solution)/shard_map/ppermute | solution.py:21
  423.2 14.8 %while.67 = (s32[]{:T(128)}, f32[512]{0:T(512)S(1)}, f32[4,512]{1,0:T(4,128)S(1)}, f32[4,512]{1,0:T(4,128)S(1)}, s32[4]{0:T(128)S(1)}, /*index=5*/f32[4,8]{1,0:T...) while((s32[]{:T(128)}, f32[512]{0:T(512)S(1)}, ...), condition=%wide.region_4.5_spmd, body=%wide.region_3.4_spmd.sunk | while | flops 3408901 | bytes 1081619 | solution.py:143
  467.7 5.7 %collective-permute-done.27 = f32[512]{0:T(512)S(1)} collective-permute-done((f32[512]{0:T(512)S(1)}, f32[512]{0:T(512)S(1)}, u32[]{:S(2)}, u32[]{:S(2)}) %collective-permute-start.27) | collective-permute-done | bytes 2080 | tf_op jit(solution)/shard_map/ppermute | solution.py:21
  507.5 33.6 %all-gather.47.cloned.1.call-done = f32[512,512]{1,0:T(8,128)} async-done(((f32[512,256]{1,0:T(8,128)}), f32[512,512]{1,0:T(8,128)}) %all-gather.47.cloned.1.call-update) | async-done | bytes 1048592 | tf_op jit(solution)/shard_map/all_gather | solution.py:109
  (359 shorter events, 244.3 us)
Async XLA Ops:
  7.2 109.4 %all-gather.19.cloned.1.call-start = ((), (), s32[]{:S(2)}) async-start(), calls=%async_computation.2 | async-start | bytes 1572864 | tf_op jit(solution)/shard_map/all_gather | solution.py:108
  64.6 22.7 %collective-permute-start.7 = (f32[512,256]{1,0:T(8,128)}, f32[512,256]{1,0:T(8,128)S(1)}, u32[]{:S(2)}, u32[]{:S(2)}) collective-permute-start(f32[512,256]{1,0:T(8,128)} %get-tuple-element.586), channel_id=1, source_target_pairs={{0,2},{2,4},{4,6},{6,8},{8,10},{10,12},{12,14},{14,16},{16,18},{18... | collective-permute-start | bytes 1572872 | tf_op jit(solution)/shard_map/ppermute | solution.py:21
  77.0 51.7 %all-gather.33.cloned.1.call-start = ((), (), s32[]{:S(2)}) async-start(), calls=%async_computation.9 | async-start | bytes 1572864 | tf_op jit(solution)/shard_map/all_gather | solution.py:109
  87.4 14.4 %collective-permute-start.8 = (f32[512,256]{1,0:T(8,128)S(1)}, f32[512,256]{1,0:T(8,128)S(1)}, u32[]{:S(2)}, u32[]{:S(2)}) collective-permute-start(f32[512,256]{1,0:T(8,128)S(1)} %collective-permute-done.7), channel_id=1, source_target_pairs={{0,2},{2,4},{4,6},{6,8},{8,10},{10,12},{12,14},{14,16},{16,18},{18... | collective-permute-start | bytes 1572872 | tf_op jit(solution)/shard_map/ppermute | solution.py:21
  102.6 63.0 %all-gather.21.cloned.1.call-start = ((), (), s32[]{:S(2)}) async-start(), calls=%async_computation.3 | async-start | bytes 1572864 | tf_op jit(solution)/shard_map/all_gather | solution.py:108
  102.6 13.9 %collective-permute-start.1 = (f32[512,256]{1,0:T(8,128)}, f32[512,256]{1,0:T(8,128)S(1)}, u32[]{:S(2)}, u32[]{:S(2)}) collective-permute-start(f32[512,256]{1,0:T(8,128)} %copy-done.16), channel_id=1, source_target_pairs={{0,2},{2,4},{4,6},{6,8},{8,10},{10,12},{12,14},{14,16},{16,18},{18... | collective-permute-start | bytes 1572872 | tf_op jit(solution)/shard_map/ppermute | solution.py:21
  119.9 56.6 %all-gather.35.cloned.1.call-start = ((), (), s32[]{:S(2)}) async-start(), calls=%async_computation.10 | async-start | bytes 1572864 | tf_op jit(solution)/shard_map/all_gather | solution.py:109
  132.7 15.4 %collective-permute-start.9 = (f32[512,256]{1,0:T(8,128)S(1)}, f32[512,256]{1,0:T(8,128)S(1)}, u32[]{:S(2)}, u32[]{:S(2)}) collective-permute-start(f32[512,256]{1,0:T(8,128)S(1)} %fusion.14), channel_id=1, source_target_pairs={{0,4},{2,6},{4,8},{6,10},{8,12},{10,14},{12,16},{14,18},{16,20},{1... | collective-permute-start | bytes 1572872 | tf_op jit(solution)/shard_map/ppermute | solution.py:21
  148.9 60.4 %all-gather.23.cloned.1.call-start = ((), (), s32[]{:S(2)}) async-start(), calls=%async_computation.4 | async-start | bytes 1572864 | tf_op jit(solution)/shard_map/all_gather | solution.py:108
  148.9 15.8 %collective-permute-start.2 = (f32[512,256]{1,0:T(8,128)S(1)}, f32[512,256]{1,0:T(8,128)S(1)}, u32[]{:S(2)}, u32[]{:S(2)}) collective-permute-start(f32[512,256]{1,0:T(8,128)S(1)} %copy-done.14), channel_id=1, source_target_pairs={{0,4},{2,6},{4,8},{6,10},{8,12},{10,14},{12,16},{14,18},{16,20},{1... | collective-permute-start | bytes 1572872 | tf_op jit(solution)/shard_map/ppermute | solution.py:21
  169.0 49.7 %all-gather.37.cloned.1.call-start = ((), (), s32[]{:S(2)}) async-start(), calls=%async_computation.11 | async-start | bytes 1572864 | tf_op jit(solution)/shard_map/all_gather | solution.py:109
  180.6 13.9 %collective-permute-start.10 = (f32[512,256]{1,0:T(8,128)S(1)}, f32[512,256]{1,0:T(8,128)}, u32[]{:S(2)}, u32[]{:S(2)}) collective-permute-start(f32[512,256]{1,0:T(8,128)S(1)} %fusion.13), channel_id=1, source_target_pairs={{0,8},{2,10},{4,12},{6,14},{8,16},{10,18},{12,20},{14,22},{16,24},... | collective-permute-start | bytes 1572872 | tf_op jit(solution)/shard_map/ppermute | solution.py:21
  194.5 60.2 %all-gather.25.cloned.1.call-start = ((), (), s32[]{:S(2)}) async-start(), calls=%async_computation.5 | async-start | bytes 1572864 | tf_op jit(solution)/shard_map/all_gather | solution.py:108
  194.6 14.7 %collective-permute-start.3 = (f32[512,256]{1,0:T(8,128)}, f32[512,256]{1,0:T(8,128)}, u32[]{:S(2)}, u32[]{:S(2)}) collective-permute-start(f32[512,256]{1,0:T(8,128)} %convolution_select_fusion.4), channel_id=1, source_target_pairs={{0,8},{2,10},{4,12},{6,14},{8,16},{10,18},{12,20},{14,22},{16,24},... | collective-permute-start | bytes 1572872 | tf_op jit(solution)/shard_map/ppermute | solution.py:21
  212.7 46.0 %all-gather.39.cloned.1.call-start = ((), (), s32[]{:S(2)}) async-start(), calls=%async_computation.12 | async-start | bytes 1572864 | tf_op jit(solution)/shard_map/all_gather | solution.py:109
  223.0 15.4 %collective-permute-start.11 = (f32[512,256]{1,0:T(8,128)S(1)}, f32[512,256]{1,0:T(8,128)}, u32[]{:S(2)}, u32[]{:S(2)}) collective-permute-start(f32[512,256]{1,0:T(8,128)S(1)} %fusion.12), channel_id=1, source_target_pairs={{0,16},{2,18},{4,20},{6,22},{8,24},{10,26},{12,28},{14,30},{16,32}... | collective-permute-start | bytes 1572872 | tf_op jit(solution)/shard_map/ppermute | solution.py:21
  238.5 52.6 %all-gather.27.cloned.1.call-start = ((), (), s32[]{:S(2)}) async-start(), calls=%async_computation.6 | async-start | bytes 1572864 | tf_op jit(solution)/shard_map/all_gather | solution.py:108
  238.5 16.2 %collective-permute-start.4 = (f32[512,256]{1,0:T(8,128)}, f32[512,256]{1,0:T(8,128)}, u32[]{:S(2)}, u32[]{:S(2)}) collective-permute-start(f32[512,256]{1,0:T(8,128)} %convolution_select_fusion.3), channel_id=1, source_target_pairs={{0,16},{2,18},{4,20},{6,22},{8,24},{10,26},{12,28},{14,30},{16,32}... | collective-permute-start | bytes 1572872 | tf_op jit(solution)/shard_map/ppermute | solution.py:21
  258.2 41.6 %all-gather.41.cloned.1.call-start = ((), (), s32[]{:S(2)}) async-start(), calls=%async_computation.13 | async-start | bytes 1572864 | tf_op jit(solution)/shard_map/all_gather | solution.py:109
  263.0 15.0 %collective-permute-start.12 = (f32[512,256]{1,0:T(8,128)S(1)}, f32[512,256]{1,0:T(8,128)}, u32[]{:S(2)}, u32[]{:S(2)}) collective-permute-start(f32[512,256]{1,0:T(8,128)S(1)} %fusion.11), channel_id=1, source_target_pairs={{0,32},{2,34},{4,36},{6,38},{8,40},{10,42},{12,44},{14,46},{16,48}... | collective-permute-start | bytes 1572872 | tf_op jit(solution)/shard_map/ppermute | solution.py:21
  278.1 81.7 %all-gather.29.cloned.1.call-start = ((), (), s32[]{:S(2)}) async-start(), calls=%async_computation.7 | async-start | bytes 1572864 | tf_op jit(solution)/shard_map/all_gather | solution.py:108
  278.1 13.0 %collective-permute-start.5 = (f32[512,256]{1,0:T(8,128)}, f32[512,256]{1,0:T(8,128)}, u32[]{:S(2)}, u32[]{:S(2)}) collective-permute-start(f32[512,256]{1,0:T(8,128)} %convolution_select_fusion.2), channel_id=1, source_target_pairs={{0,32},{2,34},{4,36},{6,38},{8,40},{10,42},{12,44},{14,46},{16,48}... | collective-permute-start | bytes 1572872 | tf_op jit(solution)/shard_map/ppermute | solution.py:21
  294.5 68.7 %all-gather.43.cloned.1.call-start = ((), (), s32[]{:S(2)}) async-start(), calls=%async_computation.14 | async-start | bytes 1572864 | tf_op jit(solution)/shard_map/all_gather | solution.py:109
  304.2 15.0 %collective-permute-start.13 = (f32[512,256]{1,0:T(8,128)S(1)}, f32[512,256]{1,0:T(8,128)}, u32[]{:S(2)}, u32[]{:S(2)}) collective-permute-start(f32[512,256]{1,0:T(8,128)S(1)} %fusion.10), channel_id=1, source_target_pairs={{0,64},{2,66},{4,68},{6,70},{8,72},{10,74},{12,76},{14,78},{16,80}... | collective-permute-start | bytes 1572872 | tf_op jit(solution)/shard_map/ppermute | solution.py:21
  319.3 101.6 %all-gather.31.cloned.1.call-start = ((), (), s32[]{:S(2)}) async-start(), calls=%async_computation.8 | async-start | bytes 1572864 | tf_op jit(solution)/shard_map/all_gather | solution.py:108
  320.3 39.5 %collective-permute-start.6 = (f32[512,256]{1,0:T(8,128)}, f32[512,256]{1,0:T(8,128)S(1)}, u32[]{:S(2)}, u32[]{:S(2)}) collective-permute-start(f32[512,256]{1,0:T(8,128)} %convolution_select_fusion.1), channel_id=1, source_target_pairs={{0,64},{2,66},{4,68},{6,70},{8,72},{10,74},{12,76},{14,78},{16,80}... | collective-permute-start | bytes 1572872 | tf_op jit(solution)/shard_map/ppermute | solution.py:21
  352.9 29.0 %collective-permute-start.18 = (f32[512]{0:T(512)S(1)}, f32[512]{0:T(512)S(1)}, u32[]{:S(2)}, u32[]{:S(2)}) collective-permute-start(f32[512]{0:T(512)S(1)} %add_select_fusion.5), channel_id=1, source_target_pairs={{0,8},{2,10},{4,12},{6,14},{8,16},{10,18},{12,20},{14,22},{16,24},... | collective-permute-start | bytes 6152 | tf_op jit(solution)/shard_map/ppermute | solution.py:21
  363.1 135.3 %all-gather.45.cloned.1.call-start = ((), (), s32[]{:S(2)}) async-start(), calls=%async_computation.15 | async-start | bytes 1572864 | tf_op jit(solution)/shard_map/all_gather | solution.py:109
  367.8 20.7 %collective-permute-start.14 = (f32[512,256]{1,0:T(8,128)S(1)}, f32[512,256]{1,0:T(8,128)}, u32[]{:S(2)}, u32[]{:S(2)}) collective-permute-start(f32[512,256]{1,0:T(8,128)S(1)} %fusion.9), channel_id=1, source_target_pairs={{0,128},{2,130},{4,132},{6,134},{8,136},{10,138},{12,140},{14,142}... | collective-permute-start | bytes 1572872 | tf_op jit(solution)/shard_map/ppermute | solution.py:21
  388.6 118.9 %all-gather.17.cloned.1.call-start = ((), (), s32[]{:S(2)}) async-start(), calls=%async_computation.1 | async-start | bytes 1572864 | tf_op jit(solution)/shard_map/all_gather | solution.py:108
  395.2 14.6 %collective-permute-start.21 = (f32[512]{0:T(512)S(1)}, f32[512]{0:T(512)S(1)}, u32[]{:S(2)}, u32[]{:S(2)}) collective-permute-start(f32[512]{0:T(512)S(1)} %add_select_fusion.2), channel_id=1, source_target_pairs={{0,64},{2,66},{4,68},{6,70},{8,72},{10,74},{12,76},{14,78},{16,80}... | collective-permute-start | bytes 6152 | tf_op jit(solution)/shard_map/ppermute | solution.py:21
  420.2 120.9 %all-gather.47.cloned.1.call-start = ((), (), s32[]{:S(2)}) async-start(), calls=%async_computation.16 | async-start | bytes 1572864 | tf_op jit(solution)/shard_map/all_gather | solution.py:109
  (58 other events, 359.4 us)
Sparse Core Ops, SparseCore 0:
  77.1 19.9 all-gather.18
  102.7 25.8 all-gather.32
  130.4 21.4 all-gather.20
  153.6 22.8 all-gather.34
  178.1 20.9 all-gather.22
  200.8 17.8 all-gather.36
  220.5 16.1 all-gather.24
  238.6 19.0 all-gather.38
  259.5 19.9 all-gather.26
  281.1 18.7 all-gather.40
  301.7 16.3 all-gather.28
  319.7 36.2 all-gather.42
  363.2 22.9 all-gather.30
  388.7 27.5 all-gather.44
  420.3 15.8 all-gather.16
  502.7 38.3 all-gather.46
